TPU v7x, 256 devices: a whole 4x4x8 slice. The times are simulated.
256 devices in a mesh: row: 8 (over x_lo, y), col: 32 (over z, x_hi, core).
Axes of the slice: x: 4 (x_hi: 2, x_lo: 2; x = x_hi * 2 + x_lo), y: 4, z: 8, core: 2. Of those that a mesh axis runs over, the one named last changes fastest.
Arguments:
- frames: bfloat16 [1024, 8192], P('col', 'row'), may hold values from -6 to 6
- cotangent: bfloat16 [1024, 8192], P('col', 'row'), may hold values from -6 to 6
- gate_weight: bfloat16 [8192, 14336], P('row', 'col'), may hold values from -0.0625 to 0.0625
- up_weight: bfloat16 [8192, 14336], P('row', 'col'), may hold values from -0.0625 to 0.0625
- down_weight: bfloat16 [14336, 8192], P('col', 'row'), may hold values from -0.046875 to 0.046875
- utt_ids: int32 [1024], replicated, may hold values from 0 to 15, never falling along the last dimension, each value on 1 to 128 neighbouring positions
- valid_len: int32 [16], replicated, may hold values from 1 to 128
- time_start: int32 [16], replicated, may hold values from 0 to 127
- time_width: int32 [16], replicated, may hold values from 0 to 32
- freq_start: int32 [16], replicated, may hold values from 0 to 8191
- freq_width: int32 [16], replicated, may hold values from 0 to 2048
Outputs:
- output: bfloat16 [1024, 8192], P('col', 'row')
- grad_frames: bfloat16 [1024, 8192], P('col', 'row')
- grad_gate: bfloat16 [8192, 14336], P('row', 'col')
- grad_up: bfloat16 [8192, 14336], P('row', 'col')
- grad_down: bfloat16 [14336, 8192], P('col', 'row')
Inputs may be any that keep to these rules, and one draw needn't show every extreme that they name: `utt_ids`: token ids never fall along the tokens; each utterance holds 1 to 128 tokens.
All inputs are finite; a program needn't handle non-finite values.
Results may differ from a plain program's by a relative error of at most 0.025.
Values may be sent and summed in bfloat16 or wider, within the bound.
No kernel may reach another device: no remote copies, remote signals or barrier semaphores. Data moves between devices by JAX's collectives and lax.ppermute only.
A program may use at most 64 MiB of HBM per device.

v0:
```python
import jax
import jax.numpy as jnp
from jax import lax
from jax.sharding import PartitionSpec as P


def span_masks(
    utt_ids,
    local_ids,
    tok_index,
    feat_index,
    valid_len,
    time_start,
    time_width,
    freq_start,
    freq_width,
):
    utt_index = jnp.arange(valid_len.shape[0], dtype=jnp.int32)
    starts = jnp.sum((utt_ids[None, :] < utt_index[:, None]).astype(jnp.int32), axis=1)
    member = (local_ids[:, None] == utt_index[None, :]).astype(jnp.int32)

    def lookup(table):
        return jnp.sum(member * table[None, :], axis=1)

    position = tok_index - lookup(starts)
    valid_rows = position < lookup(valid_len)
    time_low = lookup(time_start)
    in_time = (position >= time_low) & (position < time_low + lookup(time_width))
    freq_low = lookup(freq_start)[:, None]
    freq_high = freq_low + lookup(freq_width)[:, None]
    in_freq = (feat_index[None, :] >= freq_low) & (feat_index[None, :] < freq_high)
    keep_mask = (valid_rows & jnp.logical_not(in_time))[:, None] & jnp.logical_not(in_freq)
    return (keep_mask, valid_rows)


def shards(
    frames,
    cotangent,
    gate_weight,
    up_weight,
    down_weight,
    utt_ids,
    valid_len,
    time_start,
    time_width,
    freq_start,
    freq_width,
):
    tok_rows, feat_cols = frames.shape
    hidden_cols = gate_weight.shape[1]
    first_tok = lax.axis_index("col") * tok_rows
    first_feat = lax.axis_index("row") * feat_cols
    tok_index = first_tok + jnp.arange(tok_rows, dtype=jnp.int32)
    feat_index = first_feat + jnp.arange(feat_cols, dtype=jnp.int32)
    local_ids = lax.dynamic_slice_in_dim(utt_ids, first_tok, tok_rows)
    keep_mask, valid_rows = span_masks(
        utt_ids,
        local_ids,
        tok_index,
        feat_index,
        valid_len,
        time_start,
        time_width,
        freq_start,
        freq_width,
    )
    masked = jnp.where(keep_mask, frames, jnp.zeros_like(frames))
    cot_valid = jnp.where(valid_rows[:, None], cotangent, jnp.zeros_like(cotangent))
    contract_last = (((1,), (1,)), ((), ()))
    contract_first = (((0,), (0,)), ((), ()))
    both_all = lax.all_gather(
        jnp.concatenate([masked, cot_valid], axis=1), "col", axis=0, tiled=True
    )
    tokens_all = both_all[:, :feat_cols]
    cot_all = both_all[:, feat_cols:]
    sums = lax.psum_scatter(
        jnp.concatenate(
            [
                jnp.dot(tokens_all, gate_weight, preferred_element_type=jnp.float32),
                jnp.dot(tokens_all, up_weight, preferred_element_type=jnp.float32),
                lax.dot_general(
                    cot_all, down_weight, contract_last, preferred_element_type=jnp.float32
                ),
            ],
            axis=1,
        ).astype(jnp.bfloat16),
        "row",
        scatter_dimension=0,
        tiled=True,
    ).astype(jnp.float32)
    gate = sums[:, :hidden_cols]
    up = sums[:, hidden_cols : 2 * hidden_cols]
    grad_hidden = sums[:, 2 * hidden_cols :]
    sigmoid_gate = jax.nn.sigmoid(gate)
    hidden = (gate * sigmoid_gate * up).astype(jnp.bfloat16)
    dgate = (grad_hidden * up * sigmoid_gate * (1.0 + gate * (1.0 - sigmoid_gate))).astype(
        jnp.bfloat16
    )
    dup = (grad_hidden * gate * sigmoid_gate).astype(jnp.bfloat16)
    acts_all = lax.all_gather(
        jnp.concatenate([hidden, dgate, dup], axis=1), "row", axis=0, tiled=True
    )
    hidden_all = acts_all[:, :hidden_cols]
    dgate_all = acts_all[:, hidden_cols : 2 * hidden_cols]
    dup_all = acts_all[:, 2 * hidden_cols :]
    grad_down = lax.dot_general(
        hidden_all, cot_all, contract_first, preferred_element_type=jnp.float32
    ).astype(jnp.bfloat16)
    grad_gate = lax.dot_general(
        tokens_all, dgate_all, contract_first, preferred_element_type=jnp.float32
    ).astype(jnp.bfloat16)
    grad_up = lax.dot_general(
        tokens_all, dup_all, contract_first, preferred_element_type=jnp.float32
    ).astype(jnp.bfloat16)
    out_sums = lax.psum_scatter(
        jnp.concatenate(
            [
                jnp.dot(hidden_all, down_weight, preferred_element_type=jnp.float32).astype(
                    jnp.bfloat16
                ),
                (
                    lax.dot_general(
                        dgate_all, gate_weight, contract_last, preferred_element_type=jnp.float32
                    )
                    + lax.dot_general(
                        dup_all, up_weight, contract_last, preferred_element_type=jnp.float32
                    )
                ).astype(jnp.bfloat16),
            ],
            axis=1,
        ),
        "col",
        scatter_dimension=0,
        tiled=True,
    )
    output = out_sums[:, :feat_cols]
    grad_masked = out_sums[:, feat_cols:].astype(jnp.float32)
    grad_frames = jnp.where(keep_mask, grad_masked, jnp.zeros_like(grad_masked)).astype(
        jnp.bfloat16
    )
    return (output, grad_frames, grad_gate, grad_up, grad_down)


def solution(mesh):
    placed = (
        P("col", "row"),
        P("col", "row"),
        P("row", "col"),
        P("row", "col"),
        P("col", "row"),
        P(),
        P(),
        P(),
        P(),
        P(),
        P(),
    )
    return jax.shard_map(
        shards,
        mesh=mesh,
        in_specs=placed,
        out_specs=(
            P("col", "row"),
            P("col", "row"),
            P("row", "col"),
            P("row", "col"),
            P("col", "row"),
        ),
        check_vma=False,
    )
```

profile of v0, /device:TPU:8, one launch (start us, length us, event | category | flops | bytes accessed | tf_op | source)
XLA Modules:
  0.0 367.0 jit_solution(1127609087687936519)
XLA Ops:
  7.2 0.9 convert_reduce_fusion
  8.2 0.8 dynamic_slice.3
  8.9 1.0 copy.26
  10.0 1.0 copy.27
  11.0 0.8 select_reduce_fusion.2
  13.1 89.6 %all-gather.3.cloned.1.call-done = bf16[1024,2048]{1,0:T(8,128)(2,1)} async-done(((bf16[32,2048]{1,0:T(8,128)(2,1)}), bf16[1024,2048]{1,0:T(8,128)(2,1)}) %all-gather.3.cloned.1.call-update) | async-done | bytes 4194320 | tf_op jit(solution)/shard_map/all_gather | solution.py:71
  102.7 2.9 convolution_convert_fusion.3
  105.6 1.2 fusion.4
  106.8 1.2 convolution_convert_fusion.4
  107.9 1.8 pad_maximum_fusion.1
  109.8 4.5 %copy.32 = bf16[1024,1344]{1,0:T(8,128)(2,1)} copy(bf16[1024,1344]{0,1:T(8,128)(2,1)} %pad_maximum_fusion.1) | data formatting | bytes 5505024
  114.4 43.0 %reduce-scatter.7.cloned.1.call-done = bf16[128,1344]{1,0:T(8,128)(2,1)} async-done(((bf16[1024,1344]{1,0:T(8,128)(2,1)}), bf16[128,1344]{1,0:T(8,128)(2,1)}) %reduce-scatter.7.cloned.1.call-update) | async-done | bytes 344080
  157.4 1.2 copy.33
  159.9 54.0 %all-gather.5.cloned.1.call-done = bf16[1024,1344]{0,1:T(8,128)(2,1)} async-done(((bf16[128,1344]{0,1:T(8,128)(2,1)}), bf16[1024,1344]{0,1:T(8,128)(2,1)}) %all-gather.5.cloned.1.call-update) | async-done | bytes 2752528 | tf_op jit(solution)/shard_map/all_gather | solution.py:100
  213.8 2.6 convolution_convert_fusion
  216.5 1.4 fusion.17
  217.8 1.4 add_convert_fusion
  219.3 2.4 pad_maximum_fusion
  221.7 6.5 %copy.34 = bf16[1024,2048]{1,0:T(8,128)(2,1)} copy(bf16[1024,2048]{0,1:T(8,128)(2,1)} %pad_maximum_fusion) | data formatting | bytes 8388608
  228.3 4.1 %fusion.7 = bf16[448,1024]{1,0:T(8,128)(2,1)} fusion(bf16[1024,2048]{1,0:T(8,128)(2,1)} %all-gather.3.cloned.1.call-done, bf16[1024,1344]{0,1:T(8,128)(2,1)} %all-gather.5.cloned.1.call-done), kind=kOutput, calls=%fused_computation.9 | convolution fusion | flops 939982848 | bytes 3932160 | tf_op jit(solution)/shard_map/dot_general | solution.py:106
  232.3 2.1 convolution_convert_fusion.2
  234.4 2.0 convolution_convert_fusion.1
  236.4 121.4 %reduce-scatter.9.cloned.1.call-done = bf16[32,2048]{1,0:T(8,128)(2,1)} async-done(((bf16[1024,2048]{1,0:T(8,128)(2,1)}), bf16[32,2048]{1,0:T(8,128)(2,1)}) %reduce-scatter.9.cloned.1.call-update) | async-done | bytes 131088
  357.8 1.5 fusion.23
  (37 shorter events, 3.8 us)
Async XLA Ops:
  7.2 98.4 %copy-start = (bf16[448,1024]{1,0:T(8,128)(2,1)S(1)}, bf16[448,1024]{1,0:T(8,128)(2,1)}, u32[]{:S(2)}) copy-start(bf16[448,1024]{1,0:T(8,128)(2,1)} %param.15) | copy-start | bytes 2752516
  7.2 95.5 %copy-start.1 = (bf16[1024,448]{0,1:T(8,128)(2,1)S(1)}, bf16[1024,448]{0,1:T(8,128)(2,1)}, u32[]{:S(2)}) copy-start(bf16[1024,448]{0,1:T(8,128)(2,1)} %param.14) | copy-start | bytes 2752516
  7.2 95.5 %all-gather.3.cloned.1.call-start = ((), (), s32[]{:S(2)}) async-start(), calls=%async_computation.2 | async-start | bytes 4325376 | tf_op jit(solution)/shard_map/all_gather | solution.py:71
  13.1 144.4 %reduce-scatter.7.cloned.1.call-start = ((), (), s32[]{:S(2)}) async-start(), calls=%async_computation.4 | async-start | bytes 3244032
  102.7 2.9 copy-start.4
  105.6 1.2 copy-start.6
  114.3 99.5 %all-gather.5.cloned.1.call-start = ((), (), s32[]{:S(2)}) async-start(), calls=%async_computation.3 | async-start | bytes 3096576 | tf_op jit(solution)/shard_map/all_gather | solution.py:100
  159.6 56.8 %copy-start.7 = (bf16[1024,448]{0,1:T(8,128)(2,1)S(1)}, bf16[1024,448]{0,1:T(8,128)(2,1)}, u32[]{:S(2)}) copy-start(bf16[1024,448]{0,1:T(8,128)(2,1)} %param.13) | copy-start | bytes 2752516
  159.6 198.2 %reduce-scatter.9.cloned.1.call-start = ((), (), s32[]{:S(2)}) async-start(), calls=%async_computation.5 | async-start | bytes 4325376
  213.8 2.6 copy-start.2
  228.2 4.1 %copy-start.3 = (bf16[1024,1344]{0,1:T(8,128)(2,1)S(1)}, bf16[1024,1344]{0,1:T(8,128)(2,1)}, u32[]{:S(2)}) copy-start(bf16[1024,1344]{0,1:T(8,128)(2,1)} %all-gather.5.cloned.1.call-done) | copy-start | bytes 8257540
  228.2 4.1 %copy-start.5 = (bf16[1024,2048]{1,0:T(8,128)(2,1)S(1)}, bf16[1024,2048]{1,0:T(8,128)(2,1)}, u32[]{:S(2)}) copy-start(bf16[1024,2048]{1,0:T(8,128)(2,1)} %all-gather.3.cloned.1.call-done) | copy-start | bytes 12582916
Sparse Core Ops, SparseCore 0:
  13.2 89.4 all-gather.2
  114.5 42.9 reduce-scatter.6
  159.7 54.0 all-gather.4
  228.4 129.3 reduce-scatter.8
where the time goes:
time: 368 us; the launch traced here: 367 us
  waiting for transfers between devices  308 us (84%)
  matrix products  18.8 us (5%)
  local copies, waits for them, and re-layouts  17.7 us (5%)
  between operations  14 us (4%)
  other arithmetic  8.17 us (2%)
    unnamed x6, waiting for transfers between devices  164 us
    all_gather x1, waiting for transfers between devices, shards(): lax.all_gather(jnp.concatenate([masked, cot_valid], axis=1), 'col', axis=...  89.6 us
    all_gather x1, waiting for transfers between devices, shards(): lax.all_gather(jnp.concatenate([hidden, dgate, dup], axis=1), 'row', axis...  54 us
    unnamed x23, local copies, waits for them, and re-layouts  15.2 us
  transfers between devices with their start and end apart: 4, of which 4 were waited for; matrix products, arithmetic and copies ran while one was open for 2% of the time, Pallas kernels for 0%

commit v1 on v0

--- a/solution.py
+++ b/solution.py
@@ -97,8 +97,14 @@
         jnp.bfloat16
     )
     dup = (grad_hidden * gate * sigmoid_gate).astype(jnp.bfloat16)
-    acts_all = lax.all_gather(
-        jnp.concatenate([hidden, dgate, dup], axis=1), "row", axis=0, tiled=True
+    acts_all = jnp.concatenate(
+        lax.all_to_all(
+            jnp.stack([jnp.concatenate([hidden, dgate, dup], axis=1)] * lax.axis_size("row")),
+            "row",
+            0,
+            0,
+        ),
+        axis=0,
     )
     hidden_all = acts_all[:, :hidden_cols]
     dgate_all = acts_all[:, hidden_cols : 2 * hidden_cols]

time: 368 us -> 346 us (0.940)
  waiting for transfers between devices: 308 us -> 253 us
  blocking collectives: 0 us -> 33.9 us
    all_gather x1 -> x0, waiting for transfers between devices: 54 us -> none  [shards(): lax.all_gather(jnp.concatenate([hidden, dgate, dup], axis=1), 'row', axis...]
    all_to_all x0 -> x1, blocking collectives: none -> 33.9 us  [shards(): lax.all_to_all(jnp.stack([jnp.concatenate([hidden, dgate, dup], axis=1)]...]
    unnamed x6 -> x5, waiting for transfers between devices: 164 us -> 164 us
  transfers between devices with their start and end apart: 4 -> 3, of which waited for: 4 -> 3; matrix products, arithmetic and copies ran while one was open for 2% -> 2% of each run, Pallas kernels for 0% -> 0%
where the time goes in v1:
time: 346 us; the launch traced here: 345 us
  waiting for transfers between devices  253 us (73%)
  blocking collectives  33.9 us (10%)
  local copies, waits for them, and re-layouts  19 us (5%)
  matrix products  17.3 us (5%)
  between operations  14 us (4%)
  other arithmetic  7.45 us (2%)
    unnamed x5, waiting for transfers between devices  164 us
    all_gather x1, waiting for transfers between devices, shards(): lax.all_gather(jnp.concatenate([masked, cot_valid], axis=1), 'col', axis=...  89.6 us
    all_to_all x1, blocking collectives, shards(): lax.all_to_all(jnp.stack([jnp.concatenate([hidden, dgate, dup], axis=1)]...  33.9 us
    unnamed x23, local copies, waits for them, and re-layouts  15.7 us
  transfers between devices with their start and end apart: 3, of which 3 were waited for; matrix products, arithmetic and copies ran while one was open for 2% of the time, Pallas kernels for 0%

profile of v1, /device:TPU:8, one launch (start us, length us, event | category | flops | bytes accessed | tf_op | source)
XLA Modules:
  0.0 345.0 jit_solution(7296411597547787419)
XLA Ops:
  7.2 0.9 convert_reduce_fusion
  8.2 0.8 dynamic_slice.3
  8.9 1.0 copy.34
  10.0 1.0 copy.35
  11.0 0.8 select_reduce_fusion.2
  13.1 89.6 %all-gather.2.cloned.1.call-done = bf16[1024,2048]{1,0:T(8,128)(2,1)} async-done(((bf16[32,2048]{1,0:T(8,128)(2,1)}), bf16[1024,2048]{1,0:T(8,128)(2,1)}) %all-gather.2.cloned.1.call-update) | async-done | bytes 4194320 | tf_op jit(solution)/shard_map/all_gather | solution.py:71
  102.7 2.9 convolution_convert_fusion.3
  105.6 1.2 fusion.4
  106.8 1.2 convolution_convert_fusion.4
  107.9 1.8 pad_maximum_fusion.1
  109.8 4.5 %copy.41 = bf16[1024,1344]{1,0:T(8,128)(2,1)} copy(bf16[1024,1344]{0,1:T(8,128)(2,1)} %pad_maximum_fusion.1) | data formatting | bytes 5505024
  114.4 43.1 %reduce-scatter.7.cloned.1.call-done = bf16[128,1344]{1,0:T(8,128)(2,1)} async-done(((bf16[1024,1344]{1,0:T(8,128)(2,1)}), bf16[128,1344]{1,0:T(8,128)(2,1)}) %reduce-scatter.7.cloned.1.call-update) | async-done | bytes 344080
  157.5 1.2 copy.42
  159.3 33.9 %all_to_all.5 = bf16[8,128,1344]{1,2,0:T(8,128)(2,1)S(1)} all-to-all(bf16[8,128,1344]{1,2,0:T(8,128)(2,1)S(1)} %stack.2), channel_id=1, replica_groups=mesh['row'=8,'col'=32] {'row'}, dimensions={0} | all-to-all | bytes 5505024 | tf_op jit(solution)/shard_map/all_to_all | solution.py:101
  193.6 1.3 convolution_convert_fusion
  195.4 1.3 fusion.17
  196.7 1.3 add_convert_fusion
  198.0 2.4 pad_maximum_fusion
  200.5 6.5 %copy.43 = bf16[1024,2048]{1,0:T(8,128)(2,1)} copy(bf16[1024,2048]{0,1:T(8,128)(2,1)} %pad_maximum_fusion) | data formatting | bytes 8388608
  207.0 4.1 %fusion.7 = bf16[448,1024]{1,0:T(8,128)(2,1)} fusion(bf16[1024,2048]{1,0:T(8,128)(2,1)} %all-gather.2.cloned.1.call-done, bf16[1024,1344]{0,1:T(8,128)(2,1)} %copy-done.1), kind=kOutput, calls=%fused_computation.10 | convolution fusion | flops 939982848 | bytes 3932160 | tf_op jit(solution)/shard_map/dot_general | solution.py:112
  211.1 2.1 convolution_convert_fusion.2
  213.1 2.0 convolution_convert_fusion.1
  215.2 120.6 %reduce-scatter.9.cloned.1.call-done = bf16[32,2048]{1,0:T(8,128)(2,1)} async-done(((bf16[1024,2048]{1,0:T(8,128)(2,1)}), bf16[32,2048]{1,0:T(8,128)(2,1)}) %reduce-scatter.9.cloned.1.call-update) | async-done | bytes 131088
  335.8 1.5 fusion.23
  (37 shorter events, 4.1 us)
Async XLA Ops:
  7.2 98.4 %copy-start = (bf16[448,1024]{1,0:T(8,128)(2,1)S(1)}, bf16[448,1024]{1,0:T(8,128)(2,1)}, u32[]{:S(2)}) copy-start(bf16[448,1024]{1,0:T(8,128)(2,1)} %param.15) | copy-start | bytes 2752516
  7.2 95.5 %copy-start.3 = (bf16[1024,448]{0,1:T(8,128)(2,1)S(1)}, bf16[1024,448]{0,1:T(8,128)(2,1)}, u32[]{:S(2)}) copy-start(bf16[1024,448]{0,1:T(8,128)(2,1)} %param.14) | copy-start | bytes 2752516
  7.2 95.5 %all-gather.2.cloned.1.call-start = ((), (), s32[]{:S(2)}) async-start(), calls=%async_computation.3 | async-start | bytes 4325376 | tf_op jit(solution)/shard_map/all_gather | solution.py:71
  13.1 144.4 %reduce-scatter.7.cloned.1.call-start = ((), (), s32[]{:S(2)}) async-start(), calls=%async_computation.4 | async-start | bytes 3244032
  102.7 2.9 copy-start.4
  105.6 1.2 copy-start.6
  114.3 221.5 %reduce-scatter.9.cloned.1.call-start = ((), (), s32[]{:S(2)}) async-start(), calls=%async_computation.5 | async-start | bytes 4325376
  193.6 3.2 copy-start.1
  193.6 1.8 copy-start.7
  207.0 4.1 %copy-start.2 = (bf16[1024,1344]{0,1:T(8,128)(2,1)S(1)}, bf16[1024,1344]{0,1:T(8,128)(2,1)}, u32[]{:S(2)}) copy-start(bf16[1024,1344]{0,1:T(8,128)(2,1)} %copy-done.1) | copy-start | bytes 8257540
  207.0 4.1 %copy-start.5 = (bf16[1024,2048]{1,0:T(8,128)(2,1)S(1)}, bf16[1024,2048]{1,0:T(8,128)(2,1)}, u32[]{:S(2)}) copy-start(bf16[1024,2048]{1,0:T(8,128)(2,1)} %all-gather.2.cloned.1.call-done) | copy-start | bytes 12582916
Sparse Core Ops, SparseCore 0:
  13.2 89.4 all-gather.1
  114.5 42.9 reduce-scatter.6
  207.1 128.6 reduce-scatter.8
